TPU v7x, 512 devices: a whole 4x4x16 slice. The times are simulated.
512 devices in a mesh: expert: 64 (over x, y, z_hi, core), dp: 8 (over z_lo).
Axes of the slice: x: 4, y: 4, z: 16 (z_hi: 2, z_lo: 8; z = z_hi * 8 + z_lo), core: 2. Of those that a mesh axis runs over, the one named last changes fastest.
Arguments:
- tokens: bfloat16 [256, 2048], P('dp'), may hold values from -6 to 6
- w_gate: bfloat16 [128, 768, 2048], P('expert', 'dp'), may hold values from -2 to 2
- w_up: bfloat16 [128, 768, 2048], P('expert', 'dp'), may hold values from -2 to 2
- w_down: bfloat16 [128, 768, 2048], P('expert', 'dp'), may hold values from -2 to 2
Outputs:
- cosine: float32 [256, 128, 128], P('expert')
All inputs are finite; a program needn't handle non-finite values.
Results may differ from a plain program's by a relative error of at most 0.0014.
Values may be sent and summed in bfloat16 or wider, within the bound.
No kernel may reach another device: no remote copies, remote signals or barrier semaphores. Data moves between devices by JAX's collectives and lax.ppermute only.
A program may use at most 64 MiB of HBM per device.

v0:
```python
import jax
import jax.numpy as jnp
from jax import lax
from jax.sharding import PartitionSpec as P

BOTH = ("expert", "dp")


def z_ring_pairs(mesh, shift):
    axes = mesh.axis_names
    devs = mesh.devices.reshape(-1)
    index_of = {}
    for i, d in enumerate(devs):
        x, y, z = d.coords[:3]
        index_of[x, y, z, d.core_on_chip] = i
    z_len = 1 + max((k[2] for k in index_of))
    pairs = []
    for (x, y, z, c), i in index_of.items():
        pairs.append((i, index_of[x, y, (z + shift) % z_len, c]))
    assert axes == BOTH
    return sorted(pairs)


def gather_blocks(block, rings, n):
    k = lax.axis_index("dp")
    shifts = tuple((s for s, _ in rings))
    received = [block] + [lax.ppermute(block, BOTH, pairs) for _, pairs in rings]
    stacked = jnp.stack(received)
    source = (k - jnp.array((0,) + shifts)) % n
    ordered = jnp.take(stacked, jnp.argsort(source), axis=0)
    return ordered


def doubling_gather(block, n):
    k = lax.axis_index("dp")
    have = block[None]
    codes = [0]
    step = n // 2
    while step:
        pairs = [(i, i ^ step) for i in range(n)]
        have = jnp.concatenate([have, lax.ppermute(have, "dp", pairs)], axis=0)
        codes = codes + [c ^ step for c in codes]
        step //= 2
    where = jnp.array(codes)
    position = jnp.argsort(where)
    return jnp.take(have, position[jnp.arange(n) ^ k], axis=0)


def transpose_blocks(w, n):
    k = lax.axis_index("dp")
    width = w.shape[2] // n
    got = [lax.dynamic_slice_in_dim(w, k * width, width, axis=2)]
    for s in range(1, n):
        piece = lax.dynamic_slice_in_dim(w, (k + s) % n * width, width, axis=2)
        got.append(lax.ppermute(piece, "dp", [(i, (i + s) % n) for i in range(n)]))
    stacked = jnp.stack(got, axis=1)
    source = (k - jnp.arange(n)) % n
    ordered = jnp.take(stacked, jnp.argsort(source), axis=1)
    return ordered.reshape(w.shape[0], -1, width)


def all_reduce_dp(x, n):
    pieces = x.reshape((n, -1))
    mine = lax.all_to_all(pieces, "dp", 0, 0, tiled=True).sum(0, keepdims=True)
    spread = jnp.broadcast_to(mine, pieces.shape)
    return lax.all_to_all(spread, "dp", 0, 0, tiled=True).reshape(x.shape)


def make_shards(mesh):
    n = mesh.shape["dp"]
    half = n // 2
    shifts = tuple(range(1, half + 1)) + tuple((-s for s in range(1, n - half)))
    rings = tuple(((s, z_ring_pairs(mesh, s)) for s in shifts))
    dp_shifts = tuple(range(1, n))

    def shards(tokens, w_gate, w_up, w_down):
        c = lax.axis_index("expert") % 2
        width = tokens.shape[1] // 2
        part = lax.dynamic_slice_in_dim(tokens, c * width, width, axis=1)
        mine = gather_blocks(part, rings, n).reshape((-1, width))
        other = lax.ppermute(mine, "expert", [(i, i ^ 1) for i in range(mesh.shape["expert"])])
        low = jnp.where(c == 0, mine, other)
        high = jnp.where(c == 0, other, mine)
        block_rows = jnp.concatenate([low, high], axis=1)
        down_cols = transpose_blocks(w_down, n)
        gate = jnp.einsum("td,ehd->eth", block_rows, w_gate, preferred_element_type=jnp.float32)
        upward = jnp.einsum("td,ehd->eth", block_rows, w_up, preferred_element_type=jnp.float32)
        hidden = (jax.nn.silu(gate) * upward).astype(jnp.bfloat16)
        hidden_all = doubling_gather(hidden, n)
        outputs = jnp.einsum(
            "keth,ekhf->etf",
            hidden_all,
            down_cols.reshape(w_down.shape[0], n, -1, down_cols.shape[2]),
            preferred_element_type=jnp.float32,
        )
        features = outputs.astype(jnp.bfloat16)
        regrouped = lax.all_to_all(features, "expert", 1, 0, tiled=True)
        partial_gram = jnp.einsum(
            "etf,gtf->teg", regrouped, regrouped, preferred_element_type=jnp.float32
        )
        gram = all_reduce_dp(partial_gram, n)
        eye = jnp.eye(gram.shape[1], dtype=jnp.bool_)
        diagonal = jnp.sum(jnp.where(eye[None], gram, 0.0), axis=2)
        inverse = lax.rsqrt(diagonal + 1e-06)
        return gram * inverse[:, :, None] * inverse[:, None, :]

    return shards


def solution(mesh):
    placed = (
        P("dp", None),
        P("expert", "dp", None),
        P("expert", "dp", None),
        P("expert", "dp", None),
    )
    return jax.shard_map(
        make_shards(mesh),
        mesh=mesh,
        in_specs=placed,
        out_specs=P("expert", None, None),
        check_vma=False,
    )
```

profile of v0, /device:TPU:32, one launch (start us, length us, event | category | flops | bytes accessed | tf_op | source)
XLA Modules:
  0.0 199.1 jit_solution(7834840285856769042)
XLA Ops:
  0.0 1.0 bitcast_dynamic-update-slice_fusion.15
  1.0 3.8 %collective-permute-start = (bf16[32,1024]{1,0:T(8,128)(2,1)S(1)}, bf16[32,1024]{1,0:T(8,128)(2,1)S(1)}, u32[]{:S(2)}, u32[]{:S(2)}) collective-permute-start(bf16[32,1024]{1,0:T(8,128)(2,1)S(1)} %get-tuple-element.12), channel_id=1, source_target_pairs={{0,1},{1,2},{2,3},{3,4},{4,5},{5,6},{6,7},{7,16},{8,9},{9,10},{10,... | collective-permute-start | bytes 196616 | tf_op jit(solution)/shard_map/ppermute | solution.py:27
  4.8 6.4 %collective-permute-start.1 = (bf16[32,1024]{1,0:T(8,128)(2,1)S(1)}, bf16[32,1024]{1,0:T(8,128)(2,1)S(1)}, u32[]{:S(2)}, u32[]{:S(2)}) collective-permute-start(bf16[32,1024]{1,0:T(8,128)(2,1)S(1)} %get-tuple-element.12), channel_id=1, source_target_pairs={{0,2},{1,3},{2,4},{3,5},{4,6},{5,7},{6,16},{7,17},{8,10},{9,11},{1... | collective-permute-start | bytes 196616 | tf_op jit(solution)/shard_map/ppermute | solution.py:27
  11.2 6.5 %collective-permute-start.2 = (bf16[32,1024]{1,0:T(8,128)(2,1)S(1)}, bf16[32,1024]{1,0:T(8,128)(2,1)S(1)}, u32[]{:S(2)}, u32[]{:S(2)}) collective-permute-start(bf16[32,1024]{1,0:T(8,128)(2,1)S(1)} %get-tuple-element.12), channel_id=1, source_target_pairs={{0,3},{1,4},{2,5},{3,6},{4,7},{5,16},{6,17},{7,18},{8,11},{9,12},{... | collective-permute-start | bytes 196616 | tf_op jit(solution)/shard_map/ppermute | solution.py:27
  17.8 6.4 %collective-permute-start.3 = (bf16[32,1024]{1,0:T(8,128)(2,1)S(1)}, bf16[32,1024]{1,0:T(8,128)(2,1)S(1)}, u32[]{:S(2)}, u32[]{:S(2)}) collective-permute-start(bf16[32,1024]{1,0:T(8,128)(2,1)S(1)} %get-tuple-element.12), channel_id=1, source_target_pairs={{0,4},{1,5},{2,6},{3,7},{4,16},{5,17},{6,18},{7,19},{8,12},{9,13},... | collective-permute-start | bytes 196616 | tf_op jit(solution)/shard_map/ppermute | solution.py:27
  24.2 2.9 %collective-permute-start.4 = (bf16[32,1024]{1,0:T(8,128)(2,1)S(1)}, bf16[32,1024]{1,0:T(8,128)(2,1)S(1)}, u32[]{:S(2)}, u32[]{:S(2)}) collective-permute-start(bf16[32,1024]{1,0:T(8,128)(2,1)S(1)} %get-tuple-element.12), channel_id=1, source_target_pairs={{0,23},{1,0},{2,1},{3,2},{4,3},{5,4},{6,5},{7,6},{8,31},{9,8},{10,... | collective-permute-start | bytes 196616 | tf_op jit(solution)/shard_map/ppermute | solution.py:27
  27.2 0.7 and_select_fusion
  27.9 1.0 sort.49
  28.9 1.0 sort.50
  29.9 0.6 gather_fusion
  30.8 0.8 constant_dynamic-slice_fusion
  31.7 4.6 %collective-permute-start.5 = (bf16[32,1024]{1,0:T(8,128)(2,1)S(1)}, bf16[32,1024]{1,0:T(8,128)(2,1)S(1)}, u32[]{:S(2)}, u32[]{:S(2)}) collective-permute-start(bf16[32,1024]{1,0:T(8,128)(2,1)S(1)} %get-tuple-element.12), channel_id=1, source_target_pairs={{0,22},{1,23},{2,0},{3,1},{4,2},{5,3},{6,4},{7,5},{8,30},{9,31},{1... | collective-permute-start | bytes 196616 | tf_op jit(solution)/shard_map/ppermute | solution.py:27
  36.3 1.9 collective-permute-start.6
  38.2 3.4 %collective-permute-start.11 = (bf16[2,96,256]{2,1,0:T(8,128)(2,1)}, bf16[2,96,256]{2,1,0:T(8,128)(2,1)S(1)}, u32[]{:S(2)}, u32[]{:S(2)}) collective-permute-start(bf16[2,96,256]{2,1,0:T(8,128)(2,1)} %get-tuple-element.20), channel_id=1, source_target_pairs={{0,1},{1,2},{2,3},{3,4},{4,5},{5,6},{6,7},{7,0},{8,9},{9,10},{10,1... | collective-permute-start | bytes 294920 | tf_op jit(solution)/shard_map/ppermute | solution.py:55
  41.6 6.0 %collective-permute-start.12 = (bf16[2,96,256]{2,1,0:T(8,128)(2,1)}, bf16[2,96,256]{2,1,0:T(8,128)(2,1)S(1)}, u32[]{:S(2)}, u32[]{:S(2)}) collective-permute-start(bf16[2,96,256]{2,1,0:T(8,128)(2,1)} %get-tuple-element.19), channel_id=1, source_target_pairs={{0,2},{1,3},{2,4},{3,5},{4,6},{5,7},{6,0},{7,1},{8,10},{9,11},{10,... | collective-permute-start | bytes 294920 | tf_op jit(solution)/shard_map/ppermute | solution.py:55
  47.7 2.6 %collective-permute-start.13 = (bf16[2,96,256]{2,1,0:T(8,128)(2,1)}, bf16[2,96,256]{2,1,0:T(8,128)(2,1)S(1)}, u32[]{:S(2)}, u32[]{:S(2)}) collective-permute-start(bf16[2,96,256]{2,1,0:T(8,128)(2,1)} %get-tuple-element.18), channel_id=1, source_target_pairs={{0,3},{1,4},{2,5},{3,6},{4,7},{5,0},{6,1},{7,2},{8,11},{9,12},{10,... | collective-permute-start | bytes 294920 | tf_op jit(solution)/shard_map/ppermute | solution.py:55
  50.3 5.4 %collective-permute-start.14 = (bf16[2,96,256]{2,1,0:T(8,128)(2,1)}, bf16[2,96,256]{2,1,0:T(8,128)(2,1)S(1)}, u32[]{:S(2)}, u32[]{:S(2)}) collective-permute-start(bf16[2,96,256]{2,1,0:T(8,128)(2,1)} %get-tuple-element.17), channel_id=1, source_target_pairs={{0,4},{1,5},{2,6},{3,7},{4,0},{5,1},{6,2},{7,3},{8,12},{9,13},{10,... | collective-permute-start | bytes 294920 | tf_op jit(solution)/shard_map/ppermute | solution.py:55
  55.7 5.8 %collective-permute-start.15 = (bf16[2,96,256]{2,1,0:T(8,128)(2,1)}, bf16[2,96,256]{2,1,0:T(8,128)(2,1)S(1)}, u32[]{:S(2)}, u32[]{:S(2)}) collective-permute-start(bf16[2,96,256]{2,1,0:T(8,128)(2,1)} %get-tuple-element.16), channel_id=1, source_target_pairs={{0,5},{1,6},{2,7},{3,0},{4,1},{5,2},{6,3},{7,4},{8,13},{9,14},{10,... | collective-permute-start | bytes 294920 | tf_op jit(solution)/shard_map/ppermute | solution.py:55
  61.6 0.6 gather_fusion.1
  62.2 0.1 bitcast_select_fusion
  62.3 1.9 collective-permute-start.7
  64.3 3.5 %collective-permute-start.16 = (bf16[2,96,256]{2,1,0:T(8,128)(2,1)S(1)}, bf16[2,96,256]{2,1,0:T(8,128)(2,1)S(1)}, u32[]{:S(2)}, u32[]{:S(2)}) collective-permute-start(bf16[2,96,256]{2,1,0:T(8,128)(2,1)S(1)} %copy-done.3), channel_id=1, source_target_pairs={{0,6},{1,7},{2,0},{3,1},{4,2},{5,3},{6,4},{7,5},{8,14},{9,15},{10,... | collective-permute-start | bytes 294920 | tf_op jit(solution)/shard_map/ppermute | solution.py:55
  67.8 6.0 %collective-permute-start.17 = (bf16[2,96,256]{2,1,0:T(8,128)(2,1)S(1)}, bf16[2,96,256]{2,1,0:T(8,128)(2,1)S(1)}, u32[]{:S(2)}, u32[]{:S(2)}) collective-permute-start(bf16[2,96,256]{2,1,0:T(8,128)(2,1)S(1)} %get-tuple-element.15), channel_id=1, source_target_pairs={{0,7},{1,0},{2,1},{3,2},{4,3},{5,4},{6,5},{7,6},{8,15},{9,8},{10,9... | collective-permute-start | bytes 294920 | tf_op jit(solution)/shard_map/ppermute | solution.py:55
  73.9 0.2 broadcast_select_fusion.1
  74.1 0.5 convolution_bitcast_fusion.2
  74.6 0.6 copy-done.4
  75.2 0.5 fusion.3
  75.7 2.4 %collective-permute-start.8 = (bf16[1,2,256,96]{2,3,1,0:T(8,128)(2,1)S(1)}, bf16[1,2,256,96]{2,3,1,0:T(8,128)(2,1)S(1)}, u32[]{:S(2)}, u32[]{:S(2)}) collective-permute-start(bf16[1,2,256,96]{2,3,1,0:T(8,128)(2,1)S(1)} %fusion.3), channel_id=1, source_target_pairs={{0,4},{1,5},{2,6},{3,7},{4,0},{5,1},{6,2},{7,3},{8,12},{9,13},{10,... | collective-permute-start | bytes 294920 | tf_op jit(solution)/shard_map/ppermute | solution.py:41
  78.2 9.2 %collective-permute-done.8 = bf16[1,2,256,96]{2,3,1,0:T(8,128)(2,1)S(1)} collective-permute-done((bf16[1,2,256,96]{2,3,1,0:T(8,128)(2,1)S(1)}, bf16[1,2,256,96]{2,3,1,0:T(8,128)(2,1)S(1)}, u32[]{:S(2)}, u32[]{:S(2)}) %collective-permute-start.8) | collective-permute-done | bytes 98336 | tf_op jit(solution)/shard_map/ppermute | solution.py:41
  87.4 3.0 %collective-permute-start.9 = (bf16[2,2,256,96]{2,3,1,0:T(8,128)(2,1)S(1)}, bf16[2,2,256,96]{2,3,1,0:T(8,128)(2,1)S(1)}, u32[]{:S(2)}, u32[]{:S(2)}) collective-permute-start(bf16[2,2,256,96]{2,3,1,0:T(8,128)(2,1)S(1)} %pad_maximum_fusion.2), channel_id=1, source_target_pairs={{0,2},{1,3},{2,0},{3,1},{4,6},{5,7},{6,4},{7,5},{8,10},{9,11},{10,... | collective-permute-start | bytes 589832 | tf_op jit(solution)/shard_map/ppermute | solution.py:41
  90.5 8.6 %collective-permute-done.9 = bf16[2,2,256,96]{2,3,1,0:T(8,128)(2,1)S(1)} collective-permute-done((bf16[2,2,256,96]{2,3,1,0:T(8,128)(2,1)S(1)}, bf16[2,2,256,96]{2,3,1,0:T(8,128)(2,1)S(1)}, u32[]{:S(2)}, u32[]{:S(2)}) %collective-permute-start.9) | collective-permute-done | bytes 196640 | tf_op jit(solution)/shard_map/ppermute | solution.py:41
  99.1 5.5 %collective-permute-start.10 = (bf16[4,2,256,96]{2,3,1,0:T(8,128)(2,1)S(1)}, bf16[4,2,256,96]{2,3,1,0:T(8,128)(2,1)}, u32[]{:S(2)}, u32[]{:S(2)}) collective-permute-start(bf16[4,2,256,96]{2,3,1,0:T(8,128)(2,1)S(1)} %pad_maximum_fusion.1), channel_id=1, source_target_pairs={{0,1},{1,0},{2,3},{3,2},{4,5},{5,4},{6,7},{7,6},{8,9},{9,8},{10,11... | collective-permute-start | bytes 1179656 | tf_op jit(solution)/shard_map/ppermute | solution.py:41
  104.7 0.6 gather_fusion.3
  105.3 8.7 %collective-permute-done.10 = bf16[4,2,256,96]{2,3,1,0:T(8,128)(2,1)} collective-permute-done((bf16[4,2,256,96]{2,3,1,0:T(8,128)(2,1)S(1)}, bf16[4,2,256,96]{2,3,1,0:T(8,128)(2,1)}, u32[]{:S(2)}, u32[]{:S(2)}) %collective-permute-start.10) | collective-permute-done | bytes 393248 | tf_op jit(solution)/shard_map/ppermute | solution.py:41
  114.0 1.1 pad_maximum_fusion
  115.1 0.6 gather_fusion.2
  115.7 0.5 fusion
  116.2 0.3 copy.13
  116.5 39.1 %all_to_all.33 = bf16[2,256,256]{2,0,1:T(2,128)(2,1)S(1)} all-to-all(bf16[2,256,256]{2,0,1:T(2,128)(2,1)S(1)} %copy.13), channel_id=1, replica_groups=mesh['expert'=64,'dp'=8] {'expert'}, dimensions={1} | all-to-all | bytes 524288 | tf_op jit(solution)/shard_map/all_to_all | solution.py:97
  155.6 0.2 copy.17
  155.9 0.2 fusion.20
  156.1 19.5 %all_to_all.34 = f32[8,1,8192]{2,1,0:T(1,128)S(1)} all-to-all(f32[8,1,8192]{2,1,0:T(1,128)S(1)} %bitcast.87), channel_id=1, replica_groups=mesh['expert'=64,'dp'=8] {'dp'}, dimensions={0} | all-to-all | bytes 524288 | tf_op jit(solution)/shard_map/all_to_all | solution.py:64
  175.7 0.2 reduce_sum.18
  175.9 0.8 broadcast_in_dim.74
  176.7 5.5 %all-to-all-start.2 = ((f32[8,1,8192]{2,1,0:T(1,128)}), f32[8,1,8192]{2,1,0:T(1,128)S(1)}, u32[]{:S(2)}, u32[]{:S(2)}) async-start(f32[8,1,8192]{2,1,0:T(1,128)} %broadcast_in_dim.74), calls=%async_computation.2 | async-start | bytes 524288 | tf_op jit(solution)/shard_map/all_to_all | solution.py:66
  182.2 15.9 %all-to-all-done.2 = f32[8,1,8192]{2,1,0:T(1,128)S(1)} async-done(((f32[8,1,8192]{2,1,0:T(1,128)}), f32[8,1,8192]{2,1,0:T(1,128)S(1)}, u32[]{:S(2)}, u32[]{:S(2)}) %all-to-all-start.2) | async-done | bytes 262176 | tf_op jit(solution)/shard_map/all_to_all | solution.py:66
  198.1 0.1 fusion.11
  198.3 0.9 fusion.12
  (59 shorter events, 0.6 us)
Async XLA Ops:
  0.0 74.0 %copy-start = (bf16[2,96,2048]{2,1,0:T(8,128)(2,1)S(1)}, bf16[2,96,2048]{2,1,0:T(8,128)(2,1)}, u32[]{:S(2)}) copy-start(bf16[2,96,2048]{2,1,0:T(8,128)(2,1)} %param.7) | copy-start | bytes 2359300
  0.0 29.9 %copy-start.1 = (s32[8]{0:T(128)S(1)}, s32[8]{0:T(128)}, u32[]{:S(2)}) copy-start(s32[8]{0:T(128)} %constant.142) | copy-start | bytes 100
  0.0 30.7 %copy-start.2 = (bf16[2,96,2048]{2,1,0:T(8,128)(2,1)S(1)}, bf16[2,96,2048]{2,1,0:T(8,128)(2,1)}, u32[]{:S(2)}) copy-start(bf16[2,96,2048]{2,1,0:T(8,128)(2,1)} %param.9) | copy-start | bytes 2359300
  1.0 30.6 %collective-permute-start = (bf16[32,1024]{1,0:T(8,128)(2,1)S(1)}, bf16[32,1024]{1,0:T(8,128)(2,1)S(1)}, u32[]{:S(2)}, u32[]{:S(2)}) collective-permute-start(bf16[32,1024]{1,0:T(8,128)(2,1)S(1)} %get-tuple-element.12), channel_id=1, source_target_pairs={{0,1},{1,2},{2,3},{3,4},{4,5},{5,6},{6,7},{7,16},{8,9},{9,10},{10,... | collective-permute-start | bytes 196616 | tf_op jit(solution)/shard_map/ppermute | solution.py:27
  4.8 31.4 %collective-permute-start.1 = (bf16[32,1024]{1,0:T(8,128)(2,1)S(1)}, bf16[32,1024]{1,0:T(8,128)(2,1)S(1)}, u32[]{:S(2)}, u32[]{:S(2)}) collective-permute-start(bf16[32,1024]{1,0:T(8,128)(2,1)S(1)} %get-tuple-element.12), channel_id=1, source_target_pairs={{0,2},{1,3},{2,4},{3,5},{4,6},{5,7},{6,16},{7,17},{8,10},{9,11},{1... | collective-permute-start | bytes 196616 | tf_op jit(solution)/shard_map/ppermute | solution.py:27
  11.2 27.0 %collective-permute-start.2 = (bf16[32,1024]{1,0:T(8,128)(2,1)S(1)}, bf16[32,1024]{1,0:T(8,128)(2,1)S(1)}, u32[]{:S(2)}, u32[]{:S(2)}) collective-permute-start(bf16[32,1024]{1,0:T(8,128)(2,1)S(1)} %get-tuple-element.12), channel_id=1, source_target_pairs={{0,3},{1,4},{2,5},{3,6},{4,7},{5,16},{6,17},{7,18},{8,11},{9,12},{... | collective-permute-start | bytes 196616 | tf_op jit(solution)/shard_map/ppermute | solution.py:27
  17.8 23.8 %collective-permute-start.3 = (bf16[32,1024]{1,0:T(8,128)(2,1)S(1)}, bf16[32,1024]{1,0:T(8,128)(2,1)S(1)}, u32[]{:S(2)}, u32[]{:S(2)}) collective-permute-start(bf16[32,1024]{1,0:T(8,128)(2,1)S(1)} %get-tuple-element.12), channel_id=1, source_target_pairs={{0,4},{1,5},{2,6},{3,7},{4,16},{5,17},{6,18},{7,19},{8,12},{9,13},... | collective-permute-start | bytes 196616 | tf_op jit(solution)/shard_map/ppermute | solution.py:27
  24.2 23.5 %collective-permute-start.4 = (bf16[32,1024]{1,0:T(8,128)(2,1)S(1)}, bf16[32,1024]{1,0:T(8,128)(2,1)S(1)}, u32[]{:S(2)}, u32[]{:S(2)}) collective-permute-start(bf16[32,1024]{1,0:T(8,128)(2,1)S(1)} %get-tuple-element.12), channel_id=1, source_target_pairs={{0,23},{1,0},{2,1},{3,2},{4,3},{5,4},{6,5},{7,6},{8,31},{9,8},{10,... | collective-permute-start | bytes 196616 | tf_op jit(solution)/shard_map/ppermute | solution.py:27
  31.7 18.7 %collective-permute-start.5 = (bf16[32,1024]{1,0:T(8,128)(2,1)S(1)}, bf16[32,1024]{1,0:T(8,128)(2,1)S(1)}, u32[]{:S(2)}, u32[]{:S(2)}) collective-permute-start(bf16[32,1024]{1,0:T(8,128)(2,1)S(1)} %get-tuple-element.12), channel_id=1, source_target_pairs={{0,22},{1,23},{2,0},{3,1},{4,2},{5,3},{6,4},{7,5},{8,30},{9,31},{1... | collective-permute-start | bytes 196616 | tf_op jit(solution)/shard_map/ppermute | solution.py:27
  36.3 19.5 %collective-permute-start.6 = (bf16[32,1024]{1,0:T(8,128)(2,1)S(1)}, bf16[32,1024]{1,0:T(8,128)(2,1)S(1)}, u32[]{:S(2)}, u32[]{:S(2)}) collective-permute-start(bf16[32,1024]{1,0:T(8,128)(2,1)S(1)} %get-tuple-element.12), channel_id=1, source_target_pairs={{0,21},{1,22},{2,23},{3,0},{4,1},{5,2},{6,3},{7,4},{8,29},{9,30},{... | collective-permute-start | bytes 196616 | tf_op jit(solution)/shard_map/ppermute | solution.py:27
  38.2 24.1 %collective-permute-start.11 = (bf16[2,96,256]{2,1,0:T(8,128)(2,1)}, bf16[2,96,256]{2,1,0:T(8,128)(2,1)S(1)}, u32[]{:S(2)}, u32[]{:S(2)}) collective-permute-start(bf16[2,96,256]{2,1,0:T(8,128)(2,1)} %get-tuple-element.20), channel_id=1, source_target_pairs={{0,1},{1,2},{2,3},{3,4},{4,5},{5,6},{6,7},{7,0},{8,9},{9,10},{10,1... | collective-permute-start | bytes 294920 | tf_op jit(solution)/shard_map/ppermute | solution.py:55
  41.6 22.7 %collective-permute-start.12 = (bf16[2,96,256]{2,1,0:T(8,128)(2,1)}, bf16[2,96,256]{2,1,0:T(8,128)(2,1)S(1)}, u32[]{:S(2)}, u32[]{:S(2)}) collective-permute-start(bf16[2,96,256]{2,1,0:T(8,128)(2,1)} %get-tuple-element.19), channel_id=1, source_target_pairs={{0,2},{1,3},{2,4},{3,5},{4,6},{5,7},{6,0},{7,1},{8,10},{9,11},{10,... | collective-permute-start | bytes 294920 | tf_op jit(solution)/shard_map/ppermute | solution.py:55
  47.7 20.1 %collective-permute-start.13 = (bf16[2,96,256]{2,1,0:T(8,128)(2,1)}, bf16[2,96,256]{2,1,0:T(8,128)(2,1)S(1)}, u32[]{:S(2)}, u32[]{:S(2)}) collective-permute-start(bf16[2,96,256]{2,1,0:T(8,128)(2,1)} %get-tuple-element.18), channel_id=1, source_target_pairs={{0,3},{1,4},{2,5},{3,6},{4,7},{5,0},{6,1},{7,2},{8,11},{9,12},{10,... | collective-permute-start | bytes 294920 | tf_op jit(solution)/shard_map/ppermute | solution.py:55
  50.3 27.8 %collective-permute-start.14 = (bf16[2,96,256]{2,1,0:T(8,128)(2,1)}, bf16[2,96,256]{2,1,0:T(8,128)(2,1)S(1)}, u32[]{:S(2)}, u32[]{:S(2)}) collective-permute-start(bf16[2,96,256]{2,1,0:T(8,128)(2,1)} %get-tuple-element.17), channel_id=1, source_target_pairs={{0,4},{1,5},{2,6},{3,7},{4,0},{5,1},{6,2},{7,3},{8,12},{9,13},{10,... | collective-permute-start | bytes 294920 | tf_op jit(solution)/shard_map/ppermute | solution.py:55
  55.7 34.7 %collective-permute-start.15 = (bf16[2,96,256]{2,1,0:T(8,128)(2,1)}, bf16[2,96,256]{2,1,0:T(8,128)(2,1)S(1)}, u32[]{:S(2)}, u32[]{:S(2)}) collective-permute-start(bf16[2,96,256]{2,1,0:T(8,128)(2,1)} %get-tuple-element.16), channel_id=1, source_target_pairs={{0,5},{1,6},{2,7},{3,0},{4,1},{5,2},{6,3},{7,4},{8,13},{9,14},{10,... | collective-permute-start | bytes 294920 | tf_op jit(solution)/shard_map/ppermute | solution.py:55
  62.2 2.1 %copy-start.3 = (bf16[2,96,256]{2,1,0:T(8,128)(2,1)S(1)}, bf16[2,96,256]{2,1,0:T(8,128)(2,1)}, u32[]{:S(2)}) copy-start(bf16[2,96,256]{2,1,0:T(8,128)(2,1)} %get-tuple-element.21) | copy-start | bytes 294916
  62.3 11.5 %collective-permute-start.7 = (bf16[256,1024]{1,0:T(8,128)(2,1)S(1)}, bf16[256,1024]{1,0:T(8,128)(2,1)S(1)}, u32[]{:S(2)}, u32[]{:S(2)}) collective-permute-start(bf16[256,1024]{1,0:T(8,128)(2,1)S(1)} %bitcast_select_fusion), channel_id=1, source_target_pairs={{0,8},{8,0},{16,24},{24,16},{32,40},{40,32},{48,56},{56,48},{64,72... | collective-permute-start | bytes 1572872 | tf_op jit(solution)/shard_map/ppermute | solution.py:81
  64.3 40.4 %collective-permute-start.16 = (bf16[2,96,256]{2,1,0:T(8,128)(2,1)S(1)}, bf16[2,96,256]{2,1,0:T(8,128)(2,1)S(1)}, u32[]{:S(2)}, u32[]{:S(2)}) collective-permute-start(bf16[2,96,256]{2,1,0:T(8,128)(2,1)S(1)} %copy-done.3), channel_id=1, source_target_pairs={{0,6},{1,7},{2,0},{3,1},{4,2},{5,3},{6,4},{7,5},{8,14},{9,15},{10,... | collective-permute-start | bytes 294920 | tf_op jit(solution)/shard_map/ppermute | solution.py:55
  67.8 36.9 %collective-permute-start.17 = (bf16[2,96,256]{2,1,0:T(8,128)(2,1)S(1)}, bf16[2,96,256]{2,1,0:T(8,128)(2,1)S(1)}, u32[]{:S(2)}, u32[]{:S(2)}) collective-permute-start(bf16[2,96,256]{2,1,0:T(8,128)(2,1)S(1)} %get-tuple-element.15), channel_id=1, source_target_pairs={{0,7},{1,0},{2,1},{3,2},{4,3},{5,4},{6,5},{7,6},{8,15},{9,8},{10,9... | collective-permute-start | bytes 294920 | tf_op jit(solution)/shard_map/ppermute | solution.py:55
  74.1 1.1 copy-start.4
  75.7 11.7 %collective-permute-start.8 = (bf16[1,2,256,96]{2,3,1,0:T(8,128)(2,1)S(1)}, bf16[1,2,256,96]{2,3,1,0:T(8,128)(2,1)S(1)}, u32[]{:S(2)}, u32[]{:S(2)}) collective-permute-start(bf16[1,2,256,96]{2,3,1,0:T(8,128)(2,1)S(1)} %fusion.3), channel_id=1, source_target_pairs={{0,4},{1,5},{2,6},{3,7},{4,0},{5,1},{6,2},{7,3},{8,12},{9,13},{10,... | collective-permute-start | bytes 294920 | tf_op jit(solution)/shard_map/ppermute | solution.py:41
  87.4 11.6 %collective-permute-start.9 = (bf16[2,2,256,96]{2,3,1,0:T(8,128)(2,1)S(1)}, bf16[2,2,256,96]{2,3,1,0:T(8,128)(2,1)S(1)}, u32[]{:S(2)}, u32[]{:S(2)}) collective-permute-start(bf16[2,2,256,96]{2,3,1,0:T(8,128)(2,1)S(1)} %pad_maximum_fusion.2), channel_id=1, source_target_pairs={{0,2},{1,3},{2,0},{3,1},{4,6},{5,7},{6,4},{7,5},{8,10},{9,11},{10,... | collective-permute-start | bytes 589832 | tf_op jit(solution)/shard_map/ppermute | solution.py:41
  99.1 14.9 %collective-permute-start.10 = (bf16[4,2,256,96]{2,3,1,0:T(8,128)(2,1)S(1)}, bf16[4,2,256,96]{2,3,1,0:T(8,128)(2,1)}, u32[]{:S(2)}, u32[]{:S(2)}) collective-permute-start(bf16[4,2,256,96]{2,3,1,0:T(8,128)(2,1)S(1)} %pad_maximum_fusion.1), channel_id=1, source_target_pairs={{0,1},{1,0},{2,3},{3,2},{4,5},{5,4},{6,7},{7,6},{8,9},{9,8},{10,11... | collective-permute-start | bytes 1179656 | tf_op jit(solution)/shard_map/ppermute | solution.py:41
  176.7 21.4 %all-to-all-start.2 = ((f32[8,1,8192]{2,1,0:T(1,128)}), f32[8,1,8192]{2,1,0:T(1,128)S(1)}, u32[]{:S(2)}, u32[]{:S(2)}) async-start(f32[8,1,8192]{2,1,0:T(1,128)} %broadcast_in_dim.74), calls=%async_computation.2 | async-start | bytes 524288 | tf_op jit(solution)/shard_map/all_to_all | solution.py:66
where the time goes:
time: 200 us; the launch traced here: 199 us
  starting transfers between devices  83.7 us (42%)
  blocking collectives  58.6 us (29%)
  waiting for transfers between devices  42.5 us (21%)
  local copies, waits for them, and re-layouts  6.55 us (3%)
  other arithmetic  5.31 us (3%)
    all_to_all x1, blocking collectives, shards(): regrouped = lax.all_to_all(features, 'expert', 1, 0, tiled=True)  39.1 us
    ppermute x7, starting transfers between devices, transpose_blocks(): got.append(lax.ppermute(piece, 'dp', [(i, (i + s) % n) for i in range(n)]))  32.7 us
    ppermute x7, starting transfers between devices, gather_blocks(): lax.ppermute(block, BOTH, pairs)  32.6 us
    ppermute x3, waiting for transfers between devices, doubling_gather(): have = jnp.concatenate([have, lax.ppermute(have, 'dp', pairs)], axis=0)  26.6 us
    all_to_all x1, blocking collectives, all_reduce_dp(): mine = lax.all_to_all(pieces, 'dp', 0, 0, tiled=True).sum(0, keepdims=True)  19.5 us
    all_to_all x1, waiting for transfers between devices, all_reduce_dp(): return lax.all_to_all(spread, 'dp', 0, 0, tiled=True).reshape(x.shape)  15.9 us
    ppermute x3, starting transfers between devices, doubling_gather(): have = jnp.concatenate([have, lax.ppermute(have, 'dp', pairs)], axis=0)  11 us
    all_to_all x1, starting transfers between devices, all_reduce_dp(): return lax.all_to_all(spread, 'dp', 0, 0, tiled=True).reshape(x.shape)  5.52 us
  transfers between devices with their start and end apart: 19, of which 4 were waited for; matrix products, arithmetic and copies ran while one was open for 4% of the time, Pallas kernels for 0%

commit v1 on v0

--- a/solution.py
+++ b/solution.py
@@ -94,7 +94,12 @@
             preferred_element_type=jnp.float32,
         )
         features = outputs.astype(jnp.bfloat16)
-        regrouped = lax.all_to_all(features, "expert", 1, 0, tiled=True)
+        regrouped = jnp.concatenate(
+            lax.all_to_all(
+                jnp.stack(jnp.split(features, lax.axis_size("expert"), axis=1)), "expert", 0, 0
+            ),
+            axis=0,
+        )
         partial_gram = jnp.einsum(
             "etf,gtf->teg", regrouped, regrouped, preferred_element_type=jnp.float32
         )

time: 200 us -> 200 us (level)
  no operation moved by 1% of the time
where the time goes in v1:
time: 200 us
  starting transfers between devices  83.7 us (42%)
  blocking collectives  58.6 us (29%)
  waiting for transfers between devices  42.5 us (21%)
  local copies, waits for them, and re-layouts  6.78 us (3%)
  other arithmetic  5.31 us (3%)
    all_to_all x1, blocking collectives, shards(): lax.all_to_all(jnp.stack(jnp.split(features, lax.axis_size('expert'), axi...  39.1 us
    ppermute x7, starting transfers between devices, transpose_blocks(): got.append(lax.ppermute(piece, 'dp', [(i, (i + s) % n) for i in range(n)]))  32.7 us
    ppermute x7, starting transfers between devices, gather_blocks(): lax.ppermute(block, BOTH, pairs)  32.6 us
    ppermute x3, waiting for transfers between devices, doubling_gather(): have = jnp.concatenate([have, lax.ppermute(have, 'dp', pairs)], axis=0)  26.6 us
    all_to_all x1, blocking collectives, all_reduce_dp(): mine = lax.all_to_all(pieces, 'dp', 0, 0, tiled=True).sum(0, keepdims=True)  19.5 us
    all_to_all x1, waiting for transfers between devices, all_reduce_dp(): return lax.all_to_all(spread, 'dp', 0, 0, tiled=True).reshape(x.shape)  15.9 us
    ppermute x3, starting transfers between devices, doubling_gather(): have = jnp.concatenate([have, lax.ppermute(have, 'dp', pairs)], axis=0)  11 us
    all_to_all x1, starting transfers between devices, all_reduce_dp(): return lax.all_to_all(spread, 'dp', 0, 0, tiled=True).reshape(x.shape)  5.52 us
  transfers between devices with their start and end apart: 19, of which 4 were waited for; matrix products, arithmetic and copies ran while one was open for 4% of the time, Pallas kernels for 0%

profile of v1, /device:TPU:32, one launch (start us, length us, event | category | flops | bytes accessed | tf_op | source)
XLA Modules:
  0.0 199.6 jit_solution(12331619717950925229)
XLA Ops:
  0.0 1.0 constant_dynamic-update-slice_fusion.7
  1.0 3.8 %collective-permute-start = (bf16[32,1024]{1,0:T(8,128)(2,1)S(1)}, bf16[32,1024]{1,0:T(8,128)(2,1)S(1)}, u32[]{:S(2)}, u32[]{:S(2)}) collective-permute-start(bf16[32,1024]{1,0:T(8,128)(2,1)S(1)} %get-tuple-element.12), channel_id=1, source_target_pairs={{0,1},{1,2},{2,3},{3,4},{4,5},{5,6},{6,7},{7,16},{8,9},{9,10},{10,... | collective-permute-start | bytes 196616 | tf_op jit(solution)/shard_map/ppermute | solution.py:27
  4.8 6.4 %collective-permute-start.1 = (bf16[32,1024]{1,0:T(8,128)(2,1)S(1)}, bf16[32,1024]{1,0:T(8,128)(2,1)S(1)}, u32[]{:S(2)}, u32[]{:S(2)}) collective-permute-start(bf16[32,1024]{1,0:T(8,128)(2,1)S(1)} %get-tuple-element.12), channel_id=1, source_target_pairs={{0,2},{1,3},{2,4},{3,5},{4,6},{5,7},{6,16},{7,17},{8,10},{9,11},{1... | collective-permute-start | bytes 196616 | tf_op jit(solution)/shard_map/ppermute | solution.py:27
  11.2 6.5 %collective-permute-start.2 = (bf16[32,1024]{1,0:T(8,128)(2,1)S(1)}, bf16[32,1024]{1,0:T(8,128)(2,1)S(1)}, u32[]{:S(2)}, u32[]{:S(2)}) collective-permute-start(bf16[32,1024]{1,0:T(8,128)(2,1)S(1)} %get-tuple-element.12), channel_id=1, source_target_pairs={{0,3},{1,4},{2,5},{3,6},{4,7},{5,16},{6,17},{7,18},{8,11},{9,12},{... | collective-permute-start | bytes 196616 | tf_op jit(solution)/shard_map/ppermute | solution.py:27
  17.8 6.4 %collective-permute-start.3 = (bf16[32,1024]{1,0:T(8,128)(2,1)S(1)}, bf16[32,1024]{1,0:T(8,128)(2,1)S(1)}, u32[]{:S(2)}, u32[]{:S(2)}) collective-permute-start(bf16[32,1024]{1,0:T(8,128)(2,1)S(1)} %get-tuple-element.12), channel_id=1, source_target_pairs={{0,4},{1,5},{2,6},{3,7},{4,16},{5,17},{6,18},{7,19},{8,12},{9,13},... | collective-permute-start | bytes 196616 | tf_op jit(solution)/shard_map/ppermute | solution.py:27
  24.2 2.9 %collective-permute-start.4 = (bf16[32,1024]{1,0:T(8,128)(2,1)S(1)}, bf16[32,1024]{1,0:T(8,128)(2,1)S(1)}, u32[]{:S(2)}, u32[]{:S(2)}) collective-permute-start(bf16[32,1024]{1,0:T(8,128)(2,1)S(1)} %get-tuple-element.12), channel_id=1, source_target_pairs={{0,23},{1,0},{2,1},{3,2},{4,3},{5,4},{6,5},{7,6},{8,31},{9,8},{10,... | collective-permute-start | bytes 196616 | tf_op jit(solution)/shard_map/ppermute | solution.py:27
  27.2 0.7 and_select_fusion
  27.9 1.0 sort.49
  28.9 1.0 sort.50
  29.9 0.6 gather_fusion
  30.6 0.1 broadcast_in_dim.64
  30.6 0.1 broadcast_in_dim.65
  30.8 0.8 constant_dynamic-slice_fusion
  31.7 4.6 %collective-permute-start.5 = (bf16[32,1024]{1,0:T(8,128)(2,1)S(1)}, bf16[32,1024]{1,0:T(8,128)(2,1)S(1)}, u32[]{:S(2)}, u32[]{:S(2)}) collective-permute-start(bf16[32,1024]{1,0:T(8,128)(2,1)S(1)} %get-tuple-element.12), channel_id=1, source_target_pairs={{0,22},{1,23},{2,0},{3,1},{4,2},{5,3},{6,4},{7,5},{8,30},{9,31},{1... | collective-permute-start | bytes 196616 | tf_op jit(solution)/shard_map/ppermute | solution.py:27
  36.3 1.9 collective-permute-start.6
  38.2 3.4 %collective-permute-start.11 = (bf16[2,96,256]{2,1,0:T(8,128)(2,1)}, bf16[2,96,256]{2,1,0:T(8,128)(2,1)S(1)}, u32[]{:S(2)}, u32[]{:S(2)}) collective-permute-start(bf16[2,96,256]{2,1,0:T(8,128)(2,1)} %get-tuple-element.20), channel_id=1, source_target_pairs={{0,1},{1,2},{2,3},{3,4},{4,5},{5,6},{6,7},{7,0},{8,9},{9,10},{10,1... | collective-permute-start | bytes 294920 | tf_op jit(solution)/shard_map/ppermute | solution.py:55
  41.6 6.0 %collective-permute-start.12 = (bf16[2,96,256]{2,1,0:T(8,128)(2,1)}, bf16[2,96,256]{2,1,0:T(8,128)(2,1)S(1)}, u32[]{:S(2)}, u32[]{:S(2)}) collective-permute-start(bf16[2,96,256]{2,1,0:T(8,128)(2,1)} %get-tuple-element.19), channel_id=1, source_target_pairs={{0,2},{1,3},{2,4},{3,5},{4,6},{5,7},{6,0},{7,1},{8,10},{9,11},{10,... | collective-permute-start | bytes 294920 | tf_op jit(solution)/shard_map/ppermute | solution.py:55
  47.7 2.6 %collective-permute-start.13 = (bf16[2,96,256]{2,1,0:T(8,128)(2,1)}, bf16[2,96,256]{2,1,0:T(8,128)(2,1)S(1)}, u32[]{:S(2)}, u32[]{:S(2)}) collective-permute-start(bf16[2,96,256]{2,1,0:T(8,128)(2,1)} %get-tuple-element.18), channel_id=1, source_target_pairs={{0,3},{1,4},{2,5},{3,6},{4,7},{5,0},{6,1},{7,2},{8,11},{9,12},{10,... | collective-permute-start | bytes 294920 | tf_op jit(solution)/shard_map/ppermute | solution.py:55
  50.3 5.4 %collective-permute-start.14 = (bf16[2,96,256]{2,1,0:T(8,128)(2,1)}, bf16[2,96,256]{2,1,0:T(8,128)(2,1)S(1)}, u32[]{:S(2)}, u32[]{:S(2)}) collective-permute-start(bf16[2,96,256]{2,1,0:T(8,128)(2,1)} %get-tuple-element.17), channel_id=1, source_target_pairs={{0,4},{1,5},{2,6},{3,7},{4,0},{5,1},{6,2},{7,3},{8,12},{9,13},{10,... | collective-permute-start | bytes 294920 | tf_op jit(solution)/shard_map/ppermute | solution.py:55
  55.7 5.8 %collective-permute-start.15 = (bf16[2,96,256]{2,1,0:T(8,128)(2,1)}, bf16[2,96,256]{2,1,0:T(8,128)(2,1)S(1)}, u32[]{:S(2)}, u32[]{:S(2)}) collective-permute-start(bf16[2,96,256]{2,1,0:T(8,128)(2,1)} %get-tuple-element.16), channel_id=1, source_target_pairs={{0,5},{1,6},{2,7},{3,0},{4,1},{5,2},{6,3},{7,4},{8,13},{9,14},{10,... | collective-permute-start | bytes 294920 | tf_op jit(solution)/shard_map/ppermute | solution.py:55
  61.6 0.6 gather_fusion.1
  62.2 0.1 bitcast_select_fusion
  62.3 1.9 collective-permute-start.7
  64.3 3.5 %collective-permute-start.16 = (bf16[2,96,256]{2,1,0:T(8,128)(2,1)S(1)}, bf16[2,96,256]{2,1,0:T(8,128)(2,1)S(1)}, u32[]{:S(2)}, u32[]{:S(2)}) collective-permute-start(bf16[2,96,256]{2,1,0:T(8,128)(2,1)S(1)} %copy-done.3), channel_id=1, source_target_pairs={{0,6},{1,7},{2,0},{3,1},{4,2},{5,3},{6,4},{7,5},{8,14},{9,15},{10,... | collective-permute-start | bytes 294920 | tf_op jit(solution)/shard_map/ppermute | solution.py:55
  67.8 6.0 %collective-permute-start.17 = (bf16[2,96,256]{2,1,0:T(8,128)(2,1)S(1)}, bf16[2,96,256]{2,1,0:T(8,128)(2,1)S(1)}, u32[]{:S(2)}, u32[]{:S(2)}) collective-permute-start(bf16[2,96,256]{2,1,0:T(8,128)(2,1)S(1)} %get-tuple-element.15), channel_id=1, source_target_pairs={{0,7},{1,0},{2,1},{3,2},{4,3},{5,4},{6,5},{7,6},{8,15},{9,8},{10,9... | collective-permute-start | bytes 294920 | tf_op jit(solution)/shard_map/ppermute | solution.py:55
  73.9 0.2 broadcast_select_fusion.1
  74.1 0.5 convolution_bitcast_fusion.2
  74.6 0.6 copy-done.4
  75.2 0.5 fusion.3
  75.7 2.4 %collective-permute-start.8 = (bf16[1,2,256,96]{2,3,1,0:T(8,128)(2,1)S(1)}, bf16[1,2,256,96]{2,3,1,0:T(8,128)(2,1)S(1)}, u32[]{:S(2)}, u32[]{:S(2)}) collective-permute-start(bf16[1,2,256,96]{2,3,1,0:T(8,128)(2,1)S(1)} %fusion.3), channel_id=1, source_target_pairs={{0,4},{1,5},{2,6},{3,7},{4,0},{5,1},{6,2},{7,3},{8,12},{9,13},{10,... | collective-permute-start | bytes 294920 | tf_op jit(solution)/shard_map/ppermute | solution.py:41
  78.2 9.2 %collective-permute-done.8 = bf16[1,2,256,96]{2,3,1,0:T(8,128)(2,1)S(1)} collective-permute-done((bf16[1,2,256,96]{2,3,1,0:T(8,128)(2,1)S(1)}, bf16[1,2,256,96]{2,3,1,0:T(8,128)(2,1)S(1)}, u32[]{:S(2)}, u32[]{:S(2)}) %collective-permute-start.8) | collective-permute-done | bytes 98336 | tf_op jit(solution)/shard_map/ppermute | solution.py:41
  87.4 3.0 %collective-permute-start.9 = (bf16[2,2,256,96]{2,3,1,0:T(8,128)(2,1)S(1)}, bf16[2,2,256,96]{2,3,1,0:T(8,128)(2,1)S(1)}, u32[]{:S(2)}, u32[]{:S(2)}) collective-permute-start(bf16[2,2,256,96]{2,3,1,0:T(8,128)(2,1)S(1)} %pad_maximum_fusion.2), channel_id=1, source_target_pairs={{0,2},{1,3},{2,0},{3,1},{4,6},{5,7},{6,4},{7,5},{8,10},{9,11},{10,... | collective-permute-start | bytes 589832 | tf_op jit(solution)/shard_map/ppermute | solution.py:41
  90.5 8.6 %collective-permute-done.9 = bf16[2,2,256,96]{2,3,1,0:T(8,128)(2,1)S(1)} collective-permute-done((bf16[2,2,256,96]{2,3,1,0:T(8,128)(2,1)S(1)}, bf16[2,2,256,96]{2,3,1,0:T(8,128)(2,1)S(1)}, u32[]{:S(2)}, u32[]{:S(2)}) %collective-permute-start.9) | collective-permute-done | bytes 196640 | tf_op jit(solution)/shard_map/ppermute | solution.py:41
  99.1 5.5 %collective-permute-start.10 = (bf16[4,2,256,96]{2,3,1,0:T(8,128)(2,1)S(1)}, bf16[4,2,256,96]{2,3,1,0:T(8,128)(2,1)}, u32[]{:S(2)}, u32[]{:S(2)}) collective-permute-start(bf16[4,2,256,96]{2,3,1,0:T(8,128)(2,1)S(1)} %pad_maximum_fusion.1), channel_id=1, source_target_pairs={{0,1},{1,0},{2,3},{3,2},{4,5},{5,4},{6,7},{7,6},{8,9},{9,8},{10,11... | collective-permute-start | bytes 1179656 | tf_op jit(solution)/shard_map/ppermute | solution.py:41
  104.7 0.6 gather_fusion.3
  105.3 8.7 %collective-permute-done.10 = bf16[4,2,256,96]{2,3,1,0:T(8,128)(2,1)} collective-permute-done((bf16[4,2,256,96]{2,3,1,0:T(8,128)(2,1)S(1)}, bf16[4,2,256,96]{2,3,1,0:T(8,128)(2,1)}, u32[]{:S(2)}, u32[]{:S(2)}) %collective-permute-start.10) | collective-permute-done | bytes 393248 | tf_op jit(solution)/shard_map/ppermute | solution.py:41
  114.0 1.1 pad_maximum_fusion
  115.1 0.6 gather_fusion.2
  115.7 0.5 fusion
  117.2 39.1 %all_to_all.20 = bf16[64,2,4,256]{3,2,1,0:T(4,128)(2,1)S(1)} all-to-all(bf16[64,2,4,256]{3,2,1,0:T(4,128)(2,1)S(1)} %constant_dynamic-update-slice_fusion.16), channel_id=1, replica_groups=mesh['expert'=64,'dp'=8] {'expert'}, dimensions={0} | all-to-all | bytes 524288 | tf_op jit(solution)/shard_map/all_to_all | solution.py:98
  156.3 0.2 fusion.13
  156.5 19.5 %all_to_all.21 = f32[8,1,8192]{2,1,0:T(1,128)S(1)} all-to-all(f32[8,1,8192]{2,1,0:T(1,128)S(1)} %bitcast.337), channel_id=1, replica_groups=mesh['expert'=64,'dp'=8] {'dp'}, dimensions={0} | all-to-all | bytes 524288 | tf_op jit(solution)/shard_map/all_to_all | solution.py:64
  176.1 0.2 reduce_sum.18
  176.3 0.8 broadcast_in_dim.74
  177.1 5.5 %all-to-all-start.2 = ((f32[8,1,8192]{2,1,0:T(1,128)}), f32[8,1,8192]{2,1,0:T(1,128)S(1)}, u32[]{:S(2)}, u32[]{:S(2)}) async-start(f32[8,1,8192]{2,1,0:T(1,128)} %broadcast_in_dim.74), calls=%async_computation.2 | async-start | bytes 524288 | tf_op jit(solution)/shard_map/all_to_all | solution.py:66
  182.7 15.9 %all-to-all-done.2 = f32[8,1,8192]{2,1,0:T(1,128)S(1)} async-done(((f32[8,1,8192]{2,1,0:T(1,128)}), f32[8,1,8192]{2,1,0:T(1,128)S(1)}, u32[]{:S(2)}, u32[]{:S(2)}) %all-to-all-start.2) | async-done | bytes 262176 | tf_op jit(solution)/shard_map/all_to_all | solution.py:66
  198.5 0.1 fusion.11
  198.7 0.9 fusion.12
  (120 shorter events, 1.1 us)
Async XLA Ops:
  0.0 74.0 %copy-start = (bf16[2,96,2048]{2,1,0:T(8,128)(2,1)S(1)}, bf16[2,96,2048]{2,1,0:T(8,128)(2,1)}, u32[]{:S(2)}) copy-start(bf16[2,96,2048]{2,1,0:T(8,128)(2,1)} %param.7) | copy-start | bytes 2359300
  0.0 29.9 %copy-start.1 = (s32[8]{0:T(128)S(1)}, s32[8]{0:T(128)}, u32[]{:S(2)}) copy-start(s32[8]{0:T(128)} %constant.142) | copy-start | bytes 100
  0.0 30.7 %copy-start.2 = (bf16[2,96,2048]{2,1,0:T(8,128)(2,1)S(1)}, bf16[2,96,2048]{2,1,0:T(8,128)(2,1)}, u32[]{:S(2)}) copy-start(bf16[2,96,2048]{2,1,0:T(8,128)(2,1)} %param.9) | copy-start | bytes 2359300
  1.0 30.6 %collective-permute-start = (bf16[32,1024]{1,0:T(8,128)(2,1)S(1)}, bf16[32,1024]{1,0:T(8,128)(2,1)S(1)}, u32[]{:S(2)}, u32[]{:S(2)}) collective-permute-start(bf16[32,1024]{1,0:T(8,128)(2,1)S(1)} %get-tuple-element.12), channel_id=1, source_target_pairs={{0,1},{1,2},{2,3},{3,4},{4,5},{5,6},{6,7},{7,16},{8,9},{9,10},{10,... | collective-permute-start | bytes 196616 | tf_op jit(solution)/shard_map/ppermute | solution.py:27
  4.8 31.4 %collective-permute-start.1 = (bf16[32,1024]{1,0:T(8,128)(2,1)S(1)}, bf16[32,1024]{1,0:T(8,128)(2,1)S(1)}, u32[]{:S(2)}, u32[]{:S(2)}) collective-permute-start(bf16[32,1024]{1,0:T(8,128)(2,1)S(1)} %get-tuple-element.12), channel_id=1, source_target_pairs={{0,2},{1,3},{2,4},{3,5},{4,6},{5,7},{6,16},{7,17},{8,10},{9,11},{1... | collective-permute-start | bytes 196616 | tf_op jit(solution)/shard_map/ppermute | solution.py:27
  11.2 27.0 %collective-permute-start.2 = (bf16[32,1024]{1,0:T(8,128)(2,1)S(1)}, bf16[32,1024]{1,0:T(8,128)(2,1)S(1)}, u32[]{:S(2)}, u32[]{:S(2)}) collective-permute-start(bf16[32,1024]{1,0:T(8,128)(2,1)S(1)} %get-tuple-element.12), channel_id=1, source_target_pairs={{0,3},{1,4},{2,5},{3,6},{4,7},{5,16},{6,17},{7,18},{8,11},{9,12},{... | collective-permute-start | bytes 196616 | tf_op jit(solution)/shard_map/ppermute | solution.py:27
  17.8 23.8 %collective-permute-start.3 = (bf16[32,1024]{1,0:T(8,128)(2,1)S(1)}, bf16[32,1024]{1,0:T(8,128)(2,1)S(1)}, u32[]{:S(2)}, u32[]{:S(2)}) collective-permute-start(bf16[32,1024]{1,0:T(8,128)(2,1)S(1)} %get-tuple-element.12), channel_id=1, source_target_pairs={{0,4},{1,5},{2,6},{3,7},{4,16},{5,17},{6,18},{7,19},{8,12},{9,13},... | collective-permute-start | bytes 196616 | tf_op jit(solution)/shard_map/ppermute | solution.py:27
  24.2 23.5 %collective-permute-start.4 = (bf16[32,1024]{1,0:T(8,128)(2,1)S(1)}, bf16[32,1024]{1,0:T(8,128)(2,1)S(1)}, u32[]{:S(2)}, u32[]{:S(2)}) collective-permute-start(bf16[32,1024]{1,0:T(8,128)(2,1)S(1)} %get-tuple-element.12), channel_id=1, source_target_pairs={{0,23},{1,0},{2,1},{3,2},{4,3},{5,4},{6,5},{7,6},{8,31},{9,8},{10,... | collective-permute-start | bytes 196616 | tf_op jit(solution)/shard_map/ppermute | solution.py:27
  31.7 18.7 %collective-permute-start.5 = (bf16[32,1024]{1,0:T(8,128)(2,1)S(1)}, bf16[32,1024]{1,0:T(8,128)(2,1)S(1)}, u32[]{:S(2)}, u32[]{:S(2)}) collective-permute-start(bf16[32,1024]{1,0:T(8,128)(2,1)S(1)} %get-tuple-element.12), channel_id=1, source_target_pairs={{0,22},{1,23},{2,0},{3,1},{4,2},{5,3},{6,4},{7,5},{8,30},{9,31},{1... | collective-permute-start | bytes 196616 | tf_op jit(solution)/shard_map/ppermute | solution.py:27
  36.3 19.5 %collective-permute-start.6 = (bf16[32,1024]{1,0:T(8,128)(2,1)S(1)}, bf16[32,1024]{1,0:T(8,128)(2,1)S(1)}, u32[]{:S(2)}, u32[]{:S(2)}) collective-permute-start(bf16[32,1024]{1,0:T(8,128)(2,1)S(1)} %get-tuple-element.12), channel_id=1, source_target_pairs={{0,21},{1,22},{2,23},{3,0},{4,1},{5,2},{6,3},{7,4},{8,29},{9,30},{... | collective-permute-start | bytes 196616 | tf_op jit(solution)/shard_map/ppermute | solution.py:27
  38.2 24.1 %collective-permute-start.11 = (bf16[2,96,256]{2,1,0:T(8,128)(2,1)}, bf16[2,96,256]{2,1,0:T(8,128)(2,1)S(1)}, u32[]{:S(2)}, u32[]{:S(2)}) collective-permute-start(bf16[2,96,256]{2,1,0:T(8,128)(2,1)} %get-tuple-element.20), channel_id=1, source_target_pairs={{0,1},{1,2},{2,3},{3,4},{4,5},{5,6},{6,7},{7,0},{8,9},{9,10},{10,1... | collective-permute-start | bytes 294920 | tf_op jit(solution)/shard_map/ppermute | solution.py:55
  41.6 22.7 %collective-permute-start.12 = (bf16[2,96,256]{2,1,0:T(8,128)(2,1)}, bf16[2,96,256]{2,1,0:T(8,128)(2,1)S(1)}, u32[]{:S(2)}, u32[]{:S(2)}) collective-permute-start(bf16[2,96,256]{2,1,0:T(8,128)(2,1)} %get-tuple-element.19), channel_id=1, source_target_pairs={{0,2},{1,3},{2,4},{3,5},{4,6},{5,7},{6,0},{7,1},{8,10},{9,11},{10,... | collective-permute-start | bytes 294920 | tf_op jit(solution)/shard_map/ppermute | solution.py:55
  47.7 20.1 %collective-permute-start.13 = (bf16[2,96,256]{2,1,0:T(8,128)(2,1)}, bf16[2,96,256]{2,1,0:T(8,128)(2,1)S(1)}, u32[]{:S(2)}, u32[]{:S(2)}) collective-permute-start(bf16[2,96,256]{2,1,0:T(8,128)(2,1)} %get-tuple-element.18), channel_id=1, source_target_pairs={{0,3},{1,4},{2,5},{3,6},{4,7},{5,0},{6,1},{7,2},{8,11},{9,12},{10,... | collective-permute-start | bytes 294920 | tf_op jit(solution)/shard_map/ppermute | solution.py:55
  50.3 27.8 %collective-permute-start.14 = (bf16[2,96,256]{2,1,0:T(8,128)(2,1)}, bf16[2,96,256]{2,1,0:T(8,128)(2,1)S(1)}, u32[]{:S(2)}, u32[]{:S(2)}) collective-permute-start(bf16[2,96,256]{2,1,0:T(8,128)(2,1)} %get-tuple-element.17), channel_id=1, source_target_pairs={{0,4},{1,5},{2,6},{3,7},{4,0},{5,1},{6,2},{7,3},{8,12},{9,13},{10,... | collective-permute-start | bytes 294920 | tf_op jit(solution)/shard_map/ppermute | solution.py:55
  55.7 34.7 %collective-permute-start.15 = (bf16[2,96,256]{2,1,0:T(8,128)(2,1)}, bf16[2,96,256]{2,1,0:T(8,128)(2,1)S(1)}, u32[]{:S(2)}, u32[]{:S(2)}) collective-permute-start(bf16[2,96,256]{2,1,0:T(8,128)(2,1)} %get-tuple-element.16), channel_id=1, source_target_pairs={{0,5},{1,6},{2,7},{3,0},{4,1},{5,2},{6,3},{7,4},{8,13},{9,14},{10,... | collective-permute-start | bytes 294920 | tf_op jit(solution)/shard_map/ppermute | solution.py:55
  62.2 2.1 %copy-start.3 = (bf16[2,96,256]{2,1,0:T(8,128)(2,1)S(1)}, bf16[2,96,256]{2,1,0:T(8,128)(2,1)}, u32[]{:S(2)}) copy-start(bf16[2,96,256]{2,1,0:T(8,128)(2,1)} %get-tuple-element.21) | copy-start | bytes 294916
  62.3 11.5 %collective-permute-start.7 = (bf16[256,1024]{1,0:T(8,128)(2,1)S(1)}, bf16[256,1024]{1,0:T(8,128)(2,1)S(1)}, u32[]{:S(2)}, u32[]{:S(2)}) collective-permute-start(bf16[256,1024]{1,0:T(8,128)(2,1)S(1)} %bitcast_select_fusion), channel_id=1, source_target_pairs={{0,8},{8,0},{16,24},{24,16},{32,40},{40,32},{48,56},{56,48},{64,72... | collective-permute-start | bytes 1572872 | tf_op jit(solution)/shard_map/ppermute | solution.py:81
  64.3 40.4 %collective-permute-start.16 = (bf16[2,96,256]{2,1,0:T(8,128)(2,1)S(1)}, bf16[2,96,256]{2,1,0:T(8,128)(2,1)S(1)}, u32[]{:S(2)}, u32[]{:S(2)}) collective-permute-start(bf16[2,96,256]{2,1,0:T(8,128)(2,1)S(1)} %copy-done.3), channel_id=1, source_target_pairs={{0,6},{1,7},{2,0},{3,1},{4,2},{5,3},{6,4},{7,5},{8,14},{9,15},{10,... | collective-permute-start | bytes 294920 | tf_op jit(solution)/shard_map/ppermute | solution.py:55
  67.8 36.9 %collective-permute-start.17 = (bf16[2,96,256]{2,1,0:T(8,128)(2,1)S(1)}, bf16[2,96,256]{2,1,0:T(8,128)(2,1)S(1)}, u32[]{:S(2)}, u32[]{:S(2)}) collective-permute-start(bf16[2,96,256]{2,1,0:T(8,128)(2,1)S(1)} %get-tuple-element.15), channel_id=1, source_target_pairs={{0,7},{1,0},{2,1},{3,2},{4,3},{5,4},{6,5},{7,6},{8,15},{9,8},{10,9... | collective-permute-start | bytes 294920 | tf_op jit(solution)/shard_map/ppermute | solution.py:55
  74.1 1.1 copy-start.4
  75.7 11.7 %collective-permute-start.8 = (bf16[1,2,256,96]{2,3,1,0:T(8,128)(2,1)S(1)}, bf16[1,2,256,96]{2,3,1,0:T(8,128)(2,1)S(1)}, u32[]{:S(2)}, u32[]{:S(2)}) collective-permute-start(bf16[1,2,256,96]{2,3,1,0:T(8,128)(2,1)S(1)} %fusion.3), channel_id=1, source_target_pairs={{0,4},{1,5},{2,6},{3,7},{4,0},{5,1},{6,2},{7,3},{8,12},{9,13},{10,... | collective-permute-start | bytes 294920 | tf_op jit(solution)/shard_map/ppermute | solution.py:41
  87.4 11.6 %collective-permute-start.9 = (bf16[2,2,256,96]{2,3,1,0:T(8,128)(2,1)S(1)}, bf16[2,2,256,96]{2,3,1,0:T(8,128)(2,1)S(1)}, u32[]{:S(2)}, u32[]{:S(2)}) collective-permute-start(bf16[2,2,256,96]{2,3,1,0:T(8,128)(2,1)S(1)} %pad_maximum_fusion.2), channel_id=1, source_target_pairs={{0,2},{1,3},{2,0},{3,1},{4,6},{5,7},{6,4},{7,5},{8,10},{9,11},{10,... | collective-permute-start | bytes 589832 | tf_op jit(solution)/shard_map/ppermute | solution.py:41
  99.1 14.9 %collective-permute-start.10 = (bf16[4,2,256,96]{2,3,1,0:T(8,128)(2,1)S(1)}, bf16[4,2,256,96]{2,3,1,0:T(8,128)(2,1)}, u32[]{:S(2)}, u32[]{:S(2)}) collective-permute-start(bf16[4,2,256,96]{2,3,1,0:T(8,128)(2,1)S(1)} %pad_maximum_fusion.1), channel_id=1, source_target_pairs={{0,1},{1,0},{2,3},{3,2},{4,5},{5,4},{6,7},{7,6},{8,9},{9,8},{10,11... | collective-permute-start | bytes 1179656 | tf_op jit(solution)/shard_map/ppermute | solution.py:41
  177.1 21.4 %all-to-all-start.2 = ((f32[8,1,8192]{2,1,0:T(1,128)}), f32[8,1,8192]{2,1,0:T(1,128)S(1)}, u32[]{:S(2)}, u32[]{:S(2)}) async-start(f32[8,1,8192]{2,1,0:T(1,128)} %broadcast_in_dim.74), calls=%async_computation.2 | async-start | bytes 524288 | tf_op jit(solution)/shard_map/all_to_all | solution.py:66
